TPU v7x, 256 devices: a whole 4x4x8 slice. The times are simulated.
256 devices in a mesh: wide: 32 (over z_hi, y, core), narrow: 8 (over z_lo, x).
Axes of the slice: x: 4, y: 4, z: 8 (z_hi: 4, z_lo: 2; z = z_hi * 2 + z_lo), core: 2. Of those that a mesh axis runs over, the one named last changes fastest.
Arguments:
- residual: bfloat16 [256, 8192], P('wide'), may hold values from -60 to 60
- norm_gain: float32 [8192], replicated, may hold values from 0.1 to 1.9
- w_query: bfloat16 [8192, 8192], P('wide', 'narrow'), may hold values from -0.0625 to 0.0625
- key_projection_weight: bfloat16 [8192, 1024], P('wide', 'narrow'), may hold values from -0.0625 to 0.0625
- value_projection_weight: bfloat16 [8192, 1024], P('wide', 'narrow'), may hold values from -0.0625 to 0.0625
- w_out: bfloat16 [8192, 8192], P('narrow', 'wide'), may hold values from -0.5 to 0.5
- cache_keys: bfloat16 [256, 8, 1024, 128], P('wide', 'narrow'), may hold values from -480 to 480
- stored_values: bfloat16 [256, 8, 1024, 128], P('wide', 'narrow'), may hold values from -24 to 24
- lengths: int32 [256], P('wide'), may hold values from 1 to 1024, as said below
- w_enc: bfloat16 [8192, 65536], P('narrow', 'wide'), may hold values from -0.0625 to 0.0625
- b_enc: float32 [65536], P('wide'), may hold values from -3 to 3
- w_dec: bfloat16 [65536, 8192], P('wide', 'narrow'), may hold values from -0.0625 to 0.0625
- b_dec: float32 [8192], P('narrow'), may hold values from -3 to 3
- clamp_index: int32 [256, 8], replicated, may hold values from 0 to 65535, as said below
- clamp_value: float32 [256, 8], replicated, may hold values from 10 to 40
Outputs:
- steered: bfloat16 [256, 8192], P('wide', 'narrow')
Inputs may be any that keep to these rules, and one draw needn't show every extreme that they name: `lengths`: row 0 has all 1024 slots filled. `clamp_index`: the 8 latents of a row are distinct.
All inputs are finite; a program needn't handle non-finite values.
Results may differ from a plain program's by a relative error of at most 0.014.
The roundings to bfloat16 on the way count: a program that leaves them out, or rounds other values in their place, can miss the bound.
Values may be sent and summed in bfloat16 or wider, within the bound.
No kernel may reach another device: no remote copies, remote signals or barrier semaphores. Data moves between devices by JAX's collectives and lax.ppermute only.
A program may use at most 64 MiB of HBM per device.

v0:
```python
import math
import jax
import jax.numpy as jnp
from jax import lax
from jax.sharding import PartitionSpec as P

HEAD_WIDTH = 128
rope_base = 500000.0


def rotary(vectors, positions):
    halfway = vectors.shape[-1] // 2
    counter = jnp.arange(halfway, dtype=jnp.float32)
    inverse = rope_base ** (-2.0 * counter / vectors.shape[-1])
    angles = positions.astype(jnp.float32)[:, None] * inverse[None, :]
    cosine = jnp.cos(angles)[:, None, :]
    sine = jnp.sin(angles)[:, None, :]
    first_half = vectors[..., :halfway]
    second_half = vectors[..., halfway:]
    return jnp.concatenate(
        [first_half * cosine - second_half * sine, second_half * cosine + first_half * sine],
        axis=-1,
    )


def clamp_latents(pre_acts, latent_first, clamp_index, clamp_value):
    columns = latent_first + jnp.arange(pre_acts.shape[1], dtype=jnp.int32)
    result = jnp.maximum(pre_acts, 0.0)
    for clamp_slot in range(clamp_index.shape[1]):
        matched = columns[None, :] == clamp_index[:, clamp_slot : clamp_slot + 1]
        result = jnp.where(matched, clamp_value[:, clamp_slot : clamp_slot + 1], result)
    return result.astype(jnp.bfloat16)


def attend(queries, key_new, value_new, cache_keys, stored_values, lengths):
    local_rows, heads_here, head_size = queries.shape
    kv_here = key_new.shape[1]
    query_group_width = heads_here // kv_here
    grouped_queries = queries.reshape(local_rows, kv_here, query_group_width, head_size)
    scaling = 1.0 / math.sqrt(head_size)
    scores = (
        jnp.einsum(
            "rkgd,rkjd->rkgj", grouped_queries, cache_keys, preferred_element_type=jnp.float32
        )
        * scaling
    )
    in_range = (
        jnp.arange(cache_keys.shape[2], dtype=jnp.int32)[None, None, None, :]
        < lengths[:, None, None, None]
    )
    scores = jnp.where(in_range, scores, -jnp.inf)
    own_score = (
        jnp.einsum("rkgd,rkd->rkg", grouped_queries, key_new, preferred_element_type=jnp.float32)
        * scaling
    )
    highest = jnp.maximum(jnp.max(scores, axis=-1), own_score)
    weights = jnp.exp(scores - highest[..., None])
    own_weight = jnp.exp(own_score - highest)
    denominator = jnp.sum(weights, axis=-1) + own_weight
    probabilities = (weights / denominator[..., None]).astype(jnp.bfloat16)
    own_prob = (own_weight / denominator).astype(jnp.bfloat16)
    blended = jnp.einsum(
        "rkgj,rkjd->rkgd", probabilities, stored_values, preferred_element_type=jnp.float32
    )
    blended = (
        blended
        + own_prob.astype(jnp.float32)[..., None] * value_new.astype(jnp.float32)[:, :, None, :]
    )
    return blended.astype(jnp.bfloat16).reshape(local_rows, heads_here * head_size)


def on_device(
    residual,
    norm_gain,
    w_query,
    key_projection_weight,
    value_projection_weight,
    w_out,
    cache_keys,
    stored_values,
    lengths,
    w_enc,
    b_enc,
    w_dec,
    b_dec,
    clamp_index,
    clamp_value,
):
    stream = residual.astype(jnp.float32)
    local_rows = residual.shape[0]
    normalized_rows = (
        stream
        * lax.rsqrt(jnp.mean(stream * stream, axis=-1, keepdims=True) + 1e-05)
        * norm_gain[None, :]
    ).astype(jnp.bfloat16)
    by_feature = lax.all_to_all(normalized_rows, "wide", split_axis=1, concat_axis=0, tiled=True)
    query_width = w_query.shape[1]
    key_width = key_projection_weight.shape[1]
    row_block = by_feature
    projected = lax.psum_scatter(
        jnp.concatenate(
            [
                jnp.dot(row_block, w_query, preferred_element_type=jnp.float32),
                jnp.dot(row_block, key_projection_weight, preferred_element_type=jnp.float32),
                jnp.dot(row_block, value_projection_weight, preferred_element_type=jnp.float32),
            ],
            axis=1,
        ),
        "wide",
        scatter_dimension=0,
        tiled=True,
    )
    heads_here = query_width // HEAD_WIDTH
    kv_here = key_width // HEAD_WIDTH
    queries = rotary(
        projected[:, :query_width].reshape(local_rows, heads_here, HEAD_WIDTH), lengths
    ).astype(jnp.bfloat16)
    key_new = rotary(
        projected[:, query_width : query_width + key_width].reshape(
            local_rows, kv_here, HEAD_WIDTH
        ),
        lengths,
    ).astype(jnp.bfloat16)
    value_new = (
        projected[:, query_width + key_width :]
        .reshape(local_rows, kv_here, HEAD_WIDTH)
        .astype(jnp.bfloat16)
    )
    attended = attend(queries, key_new, value_new, cache_keys, stored_values, lengths)
    partial_out = jnp.dot(
        lax.all_gather(attended, "wide", axis=0, tiled=True),
        w_out,
        preferred_element_type=jnp.float32,
    )
    by_row = lax.all_to_all(partial_out, "wide", split_axis=0, concat_axis=1, tiled=True)
    head_total = lax.psum_scatter(by_row, "narrow", scatter_dimension=1, tiled=True)
    width_here = w_enc.shape[0]
    narrow_index = lax.axis_index("narrow")
    own_stream = lax.dynamic_slice_in_dim(stream, narrow_index * width_here, width_here, 1)
    hidden = (own_stream + head_total).astype(jnp.bfloat16)
    partial_pre = jnp.dot(
        lax.all_gather(hidden, "wide", axis=0, tiled=True),
        w_enc,
        preferred_element_type=jnp.float32,
    )
    latents_here = w_enc.shape[1]
    latent_first = lax.axis_index("wide") * latents_here
    summed_pre = lax.psum(partial_pre, "narrow")
    activations = clamp_latents(summed_pre + b_enc[None, :], latent_first, clamp_index, clamp_value)
    row_block = activations
    rebuilt = lax.psum_scatter(
        jnp.dot(row_block, w_dec, preferred_element_type=jnp.float32),
        "wide",
        scatter_dimension=0,
        tiled=True,
    )
    return (rebuilt + b_dec[None, :]).astype(jnp.bfloat16)


def solution(mesh):
    placed = (
        P("wide", None),
        P(),
        P("wide", "narrow"),
        P("wide", "narrow"),
        P("wide", "narrow"),
        P("narrow", "wide"),
        P("wide", "narrow", None, None),
        P("wide", "narrow", None, None),
        P("wide"),
        P("narrow", "wide"),
        P("wide"),
        P("wide", "narrow"),
        P("narrow"),
        P(),
        P(),
    )
    return jax.shard_map(
        on_device, mesh=mesh, in_specs=placed, out_specs=P("wide", "narrow"), check_vma=False
    )
```

profile of v0, /device:TPU:2, one launch (start us, length us, event | category | flops | bytes accessed | tf_op | source)
XLA Modules:
  0.0 458.9 jit_solution(15226275381327403887)
XLA Ops:
  6.5 0.0 copy-start
  6.5 0.0 copy-start.4
  6.5 0.0 copy-start.5
  6.5 0.0 reduce-scatter.4.cloned.1.call-start
  6.5 1.2 multiply_reduce_fusion
  7.8 1.0 multiply_convert_fusion
  8.8 22.2 %all_to_all.38 = bf16[8,32,256]{2,0,1:T(8,128)(2,1)S(1)} all-to-all(bf16[8,32,256]{2,0,1:T(8,128)(2,1)S(1)} %bitcast.75), channel_id=1, replica_groups=mesh['wide'=32,'narrow'=8] {'wide'}, dimensions={1} | all-to-all | bytes 262144 | tf_op jit(solution)/shard_map/all_to_all | solution.py:96
  31.0 1.3 fusion.44
  32.4 0.0 copy-done.4
  32.4 0.2 fusion.40
  32.6 0.0 copy-done.5
  32.6 0.0 copy-start.9
  32.6 0.2 fusion.42
  32.8 1.2 pad_maximum_fusion
  34.0 0.0 reduce-scatter.4.cloned.1.call-update
  34.0 0.0 reduce-scatter.6.cloned.1.call-start
  34.0 0.0 copy-done.9
  34.1 0.1 iota_compare_fusion
  34.2 0.1 multiply_cosine_fusion.1
  34.3 85.1 %reduce-scatter.4.cloned.1.call-done = f32[8,1280]{1,0:T(8,128)} async-done(((f32[256,1280]{1,0:T(8,128)}), f32[8,1280]{1,0:T(8,128)}) %reduce-scatter.4.cloned.1.call-update) | async-done | bytes 40976 | tf_op jit(solution)/shard_map/reduce_scatter | solution.py:100
  119.4 0.0 copy-start.1
  119.4 0.9 slice_bitcast_fusion
  120.3 0.1 fusion.66
  120.4 0.7 slice_bitcast_fusion.1
  121.0 0.1 fusion.61
  121.2 0.1 maximum_bitcast_fusion
  121.3 0.2 fusion.56
  121.5 0.0 copy-done
  121.5 0.8 fusion.69
  122.2 0.0 copy-start.3
  122.2 0.2 fusion.39
  122.5 0.7 fusion.59
  123.1 0.0 copy-done.1
  123.1 0.0 copy-start.2
  123.1 0.4 fusion.16
  123.6 44.2 %all_gather.6 = bf16[256,1024]{1,0:T(8,128)(2,1)S(1)} all-gather(bf16[8,1024]{1,0:T(8,128)(2,1)S(1)} %bitcast.76), channel_id=1, replica_groups=mesh['wide'=32,'narrow'=8] {'wide'}, dimensions={0}, use_global_device_ids=true | all-gather | bytes 540672 | tf_op jit(solution)/shard_map/all_gather | solution.py:131
  167.8 0.0 copy-done.3
  167.8 0.3 convolution_bitcast_fusion
  168.1 17.8 %all_to_all.39 = f32[32,8,256]{2,1,0:T(8,128)} all-to-all(f32[32,8,256]{2,1,0:T(8,128)S(1)} %convolution_bitcast_fusion), channel_id=1, replica_groups=mesh['wide'=32,'narrow'=8] {'wide'}, dimensions={0} | all-to-all | bytes 524288 | tf_op jit(solution)/shard_map/all_to_all | solution.py:135
  185.9 0.0 reduce-scatter.6.cloned.1.call-update
  185.9 0.0 all-reduce.2.cloned.1.call-start
  185.9 0.0 copy-done.2
  186.0 33.6 %reduce-scatter.6.cloned.1.call-done = f32[8,1024]{1,0:T(8,128)} async-done(((f32[8,8192]{1,0:T(8,128)}), f32[8,1024]{1,0:T(8,128)}) %reduce-scatter.6.cloned.1.call-update) | async-done | bytes 32784 | tf_op jit(solution)/shard_map/reduce_scatter | solution.py:136
  219.6 0.8 add_convert_fusion.1
  220.4 46.2 %all_gather.7 = bf16[256,1024]{1,0:T(8,128)(2,1)S(1)} all-gather(bf16[8,1024]{1,0:T(8,128)(2,1)S(1)} %add_convert_fusion.1), channel_id=1, replica_groups=mesh['wide'=32,'narrow'=8] {'wide'}, dimensions={0}, use_global_device_ids=true | all-gather | bytes 540672 | tf_op jit(solution)/shard_map/all_gather | solution.py:142
  266.6 4.8 %fusion.70 = f32[256,2048]{1,0:T(8,128)} fusion(bf16[256,1024]{1,0:T(8,128)(2,1)S(1)} %all_gather.7, bf16[1024,2048]{1,0:T(8,128)(2,1)} %param.24), kind=kOutput, calls=%fused_computation.88 | convolution fusion | flops 1073741824 | bytes 6815744 | tf_op jit(solution)/shard_map/dot_general | solution.py:141
  271.4 0.0 copy-start.6
  271.4 0.0 copy-start.7
  271.4 0.0 copy-start.10
  271.4 0.0 all-reduce.2.cloned.1.call-update
  271.4 0.0 reduce-scatter.8.cloned.1.call-start
  271.5 0.6 copy-done.6
  272.1 0.0 copy-done.7
  272.1 82.1 %all-reduce.2.cloned.1.call-done = f32[256,2048]{1,0:T(8,128)} async-done(((f32[256,2048]{1,0:T(8,128)}), f32[256,2048]{1,0:T(8,128)}) %all-reduce.2.cloned.1.call-update) | async-done | bytes 2097168 | tf_op jit(solution)/shard_map/psum | solution.py:148
  354.3 0.0 copy-done.10
  354.3 0.0 copy-start.8
  354.3 6.1 %fusion.19 = f32[256,1024]{1,0:T(8,128)} fusion(bf16[2048,1024]{1,0:T(8,128)(2,1)} %param.26, f32[256,2048]{1,0:T(8,128)} %all-reduce.2.cloned.1.call-done, f32[2048]{0:T(1024)S(1)} %copy-done.10, f32[256]{0:T(256)S(1)} %bitcast.93, f32[256]{0:T(256)S(1)} %bitcast.94, f32[256]{0:T(256)S(1)} %bitcast.88, f32[256]{0:T(256)S(1)} %bitcast.89, ...), kind=kOutput, calls=%fused_computation.12 | convolution fusion | flops 1083179008 | bytes 7372800 | tf_op jit(solution)/shard_map/dot_general | solution.py:152
  360.4 0.0 reduce-scatter.8.cloned.1.call-update
  360.4 90.6 %reduce-scatter.8.cloned.1.call-done = f32[8,1024]{1,0:T(8,128)} async-done(((f32[256,1024]{1,0:T(8,128)}), f32[8,1024]{1,0:T(8,128)}) %reduce-scatter.8.cloned.1.call-update) | async-done | bytes 32784 | tf_op jit(solution)/shard_map/reduce_scatter | solution.py:151
  451.0 0.0 copy-done.8
  451.0 1.4 add_convert_fusion
  (11 shorter events, 0.1 us)
Async XLA Ops:
  6.5 114.9 %copy-start = (bf16[8,1,1024,128]{3,2,1,0:T(8,128)(2,1)S(1)}, bf16[8,1,1024,128]{3,2,1,0:T(8,128)(2,1)}, u32[]{:S(2)}) copy-start(bf16[8,1,1024,128]{3,2,1,0:T(8,128)(2,1)} %param.21) | copy-start | bytes 6291460
  6.5 25.8 %copy-start.4 = (bf16[256,128]{1,0:T(8,128)(2,1)S(1)}, bf16[256,128]{1,0:T(8,128)(2,1)}, u32[]{:S(2)}) copy-start(bf16[256,128]{1,0:T(8,128)(2,1)} %param.19) | copy-start | bytes 196612
  6.5 26.0 %copy-start.5 = (bf16[256,128]{1,0:T(8,128)(2,1)S(1)}, bf16[256,128]{1,0:T(8,128)(2,1)}, u32[]{:S(2)}) copy-start(bf16[256,128]{1,0:T(8,128)(2,1)} %param.18) | copy-start | bytes 196612
  6.5 112.8 %reduce-scatter.4.cloned.1.call-start = ((), (), s32[]{:S(2)}) async-start(), calls=%async_computation.5 | async-start | bytes 1351680 | tf_op jit(solution)/shard_map/reduce_scatter | solution.py:100
  32.6 1.5 copy-start.9
  34.0 185.6 %reduce-scatter.6.cloned.1.call-start = ((), (), s32[]{:S(2)}) async-start(), calls=%async_computation.6 | async-start | bytes 294912 | tf_op jit(solution)/shard_map/reduce_scatter | solution.py:136
  119.4 3.8 copy-start.1
  122.2 45.5 %copy-start.3 = (bf16[1024,256]{1,0:T(8,128)(2,1)S(1)}, bf16[1024,256]{1,0:T(8,128)(2,1)}, u32[]{:S(2)}) copy-start(bf16[1024,256]{1,0:T(8,128)(2,1)} %param.20) | copy-start | bytes 1572868
  123.1 62.8 %copy-start.2 = (bf16[8,8192]{1,0:T(8,128)(2,1)S(1)}, bf16[8,8192]{1,0:T(8,128)(2,1)}, u32[]{:S(2)}) copy-start(bf16[8,8192]{1,0:T(8,128)(2,1)} %param.15) | copy-start | bytes 393220
  185.9 168.4 %all-reduce.2.cloned.1.call-start = ((), (), s32[]{:S(2)}) async-start(), calls=%async_computation.7 | async-start | bytes 4194304 | tf_op jit(solution)/shard_map/psum | solution.py:148
  271.4 0.7 copy-start.6
  271.4 0.7 copy-start.7
  271.4 82.9 %copy-start.10 = (f32[2048]{0:T(1024)S(1)}, f32[2048]{0:T(1024)}, u32[]{:S(2)}) copy-start(f32[2048]{0:T(1024)} %param.25) | copy-start | bytes 24580
  271.4 179.6 %reduce-scatter.8.cloned.1.call-start = ((), (), s32[]{:S(2)}) async-start(), calls=%async_computation.8 | async-start | bytes 1081344 | tf_op jit(solution)/shard_map/reduce_scatter | solution.py:151
  354.3 96.7 %copy-start.8 = (f32[1024]{0:T(1024)S(1)}, f32[1024]{0:T(1024)}, u32[]{:S(2)}) copy-start(f32[1024]{0:T(1024)} %param.27) | copy-start | bytes 12292
Sparse Core Ops, SparseCore 0:
  34.1 85.2 reduce-scatter.3
  186.0 33.5 reduce-scatter.5
  271.5 82.6 all-reduce.1
  360.5 90.4 reduce-scatter.7
where the time goes:
time: 459 us
  waiting for transfers between devices  292 us (64%)
  blocking collectives  130 us (28%)
  matrix products  14.3 us (3%)
  between operations  13.3 us (3%)
  other arithmetic  6.94 us (2%)
    reduce_scatter x1, waiting for transfers between devices, on_device(): lax.psum_scatter(jnp.dot(row_block, w_dec, preferred_element_type=jnp.flo...  90.6 us
    reduce_scatter x1, waiting for transfers between devices, on_device(): lax.psum_scatter(jnp.concatenate([jnp.dot(row_block, w_query, preferred_e...  85.1 us
    psum x1, waiting for transfers between devices, on_device(): summed_pre = lax.psum(partial_pre, 'narrow')  82.1 us
    all_gather x1, blocking collectives, on_device(): lax.all_gather(hidden, 'wide', axis=0, tiled=True)  46.2 us
    all_gather x1, blocking collectives, on_device(): lax.all_gather(attended, 'wide', axis=0, tiled=True)  44.2 us
    reduce_scatter x1, waiting for transfers between devices, on_device(): lax.psum_scatter(by_row, 'narrow', scatter_dimension=1, tiled=True)  33.6 us
    all_to_all x1, blocking collectives, on_device(): lax.all_to_all(normalized_rows, 'wide', split_axis=1, concat_axis=0, tile...  22.2 us
    all_to_all x1, blocking collectives, on_device(): lax.all_to_all(partial_out, 'wide', split_axis=0, concat_axis=1, tiled=True)  17.8 us
  transfers between devices with their start and end apart: 4, of which 4 were waited for; matrix products, arithmetic and copies ran while one was open for 0% of the time, Pallas kernels for 0%

commit v1 on v0

--- a/solution.py
+++ b/solution.py
@@ -132,7 +132,12 @@
         w_out,
         preferred_element_type=jnp.float32,
     )
-    by_row = lax.all_to_all(partial_out, "wide", split_axis=0, concat_axis=1, tiled=True)
+    by_row = jnp.concatenate(
+        lax.all_to_all(
+            jnp.stack(jnp.split(partial_out, lax.axis_size("wide"), axis=0)), "wide", 0, 0
+        ),
+        axis=1,
+    )
     head_total = lax.psum_scatter(by_row, "narrow", scatter_dimension=1, tiled=True)
     width_here = w_enc.shape[0]
     narrow_index = lax.axis_index("narrow")

time: 459 us -> 460 us (level)
  no operation moved by 1% of the time
where the time goes in v1:
time: 460 us; the launch traced here: 459 us
  waiting for transfers between devices  292 us (63%)
  blocking collectives  131 us (28%)
  matrix products  14.3 us (3%)
  between operations  13.5 us (3%)
  other arithmetic  6.94 us (2%)
    reduce_scatter x1, waiting for transfers between devices, on_device(): lax.psum_scatter(jnp.dot(row_block, w_dec, preferred_element_type=jnp.flo...  90.6 us
    reduce_scatter x1, waiting for transfers between devices, on_device(): lax.psum_scatter(jnp.concatenate([jnp.dot(row_block, w_query, preferred_e...  85.1 us
    psum x1, waiting for transfers between devices, on_device(): summed_pre = lax.psum(partial_pre, 'narrow')  82.2 us
    all_gather x1, blocking collectives, on_device(): lax.all_gather(hidden, 'wide', axis=0, tiled=True)  46.2 us
    all_gather x1, blocking collectives, on_device(): lax.all_gather(attended, 'wide', axis=0, tiled=True)  44.3 us
    reduce_scatter x1, waiting for transfers between devices, on_device(): lax.psum_scatter(by_row, 'narrow', scatter_dimension=1, tiled=True)  33.6 us
    all_to_all x1, blocking collectives, on_device(): lax.all_to_all(normalized_rows, 'wide', split_axis=1, concat_axis=0, tile...  22.2 us
    all_to_all x1, blocking collectives, on_device(): lax.all_to_all(jnp.stack(jnp.split(partial_out, lax.axis_size('wide'), ax...  17.8 us
  transfers between devices with their start and end apart: 4, of which 4 were waited for; matrix products, arithmetic and copies ran while one was open for 0% of the time, Pallas kernels for 0%

profile of v1, /device:TPU:2, one launch (start us, length us, event | category | flops | bytes accessed | tf_op | source)
XLA Modules:
  0.0 459.4 jit_solution(610514241968140347)
XLA Ops:
  6.5 0.0 copy-start
  6.5 0.0 copy-start.4
  6.5 0.0 copy-start.5
  6.5 0.0 reduce-scatter.4.cloned.1.call-start
  6.5 1.2 multiply_reduce_fusion
  7.8 1.0 multiply_convert_fusion
  8.8 22.2 %all_to_all.24 = bf16[8,32,256]{2,0,1:T(8,128)(2,1)S(1)} all-to-all(bf16[8,32,256]{2,0,1:T(8,128)(2,1)S(1)} %bitcast.201), channel_id=1, replica_groups=mesh['wide'=32,'narrow'=8] {'wide'}, dimensions={1} | all-to-all | bytes 262144 | tf_op jit(solution)/shard_map/all_to_all | solution.py:96
  31.0 1.3 fusion.44
  32.4 0.0 copy-done.4
  32.4 0.2 fusion.40
  32.6 0.0 copy-done.5
  32.6 0.0 copy-start.9
  32.6 0.2 fusion.42
  32.8 1.2 pad_maximum_fusion
  34.0 0.0 reduce-scatter.4.cloned.1.call-update
  34.0 0.0 reduce-scatter.6.cloned.1.call-start
  34.0 0.0 copy-done.9
  34.1 0.1 iota_compare_fusion
  34.2 0.1 multiply_cosine_fusion.1
  34.3 85.1 %reduce-scatter.4.cloned.1.call-done = f32[8,1280]{1,0:T(8,128)} async-done(((f32[256,1280]{1,0:T(8,128)}), f32[8,1280]{1,0:T(8,128)}) %reduce-scatter.4.cloned.1.call-update) | async-done | bytes 40976 | tf_op jit(solution)/shard_map/reduce_scatter | solution.py:100
  119.4 0.0 copy-start.1
  119.4 0.9 slice_bitcast_fusion
  120.3 0.1 fusion.66
  120.4 0.7 slice_bitcast_fusion.33
  121.0 0.1 fusion.61
  121.2 0.1 maximum_bitcast_fusion
  121.3 0.2 fusion.56
  121.5 0.0 copy-done
  121.5 0.8 fusion.69
  122.2 0.0 copy-start.3
  122.2 0.2 fusion.39
  122.5 0.7 fusion.59
  123.1 0.0 copy-done.1
  123.1 0.4 fusion.16
  123.6 0.0 copy-start.2
  123.6 44.3 %all_gather.6 = bf16[256,1024]{1,0:T(8,128)(2,1)S(1)} all-gather(bf16[8,1024]{1,0:T(8,128)(2,1)S(1)} %bitcast.202), channel_id=1, replica_groups=mesh['wide'=32,'narrow'=8] {'wide'}, dimensions={0}, use_global_device_ids=true | all-gather | bytes 540672 | tf_op jit(solution)/shard_map/all_gather | solution.py:131
  167.9 0.0 copy-done.3
  167.9 0.3 fusion.70
  168.6 17.8 %all_to_all.25 = f32[32,8,256]{2,1,0:T(8,128)} all-to-all(f32[32,8,256]{2,1,0:T(8,128)S(1)} %constant_dynamic-update-slice_fusion), channel_id=1, replica_groups=mesh['wide'=32,'narrow'=8] {'wide'}, dimensions={0} | all-to-all | bytes 524288 | tf_op jit(solution)/shard_map/all_to_all | solution.py:136
  186.4 0.0 reduce-scatter.6.cloned.1.call-update
  186.4 0.0 all-reduce.2.cloned.1.call-start
  186.4 0.0 copy-done.2
  186.5 33.6 %reduce-scatter.6.cloned.1.call-done = f32[8,1024]{1,0:T(8,128)} async-done(((f32[8,8192]{1,0:T(8,128)}), f32[8,1024]{1,0:T(8,128)}) %reduce-scatter.6.cloned.1.call-update) | async-done | bytes 32784 | tf_op jit(solution)/shard_map/reduce_scatter | solution.py:141
  220.1 0.8 add_convert_fusion.1
  220.8 46.2 %all_gather.7 = bf16[256,1024]{1,0:T(8,128)(2,1)S(1)} all-gather(bf16[8,1024]{1,0:T(8,128)(2,1)S(1)} %add_convert_fusion.1), channel_id=1, replica_groups=mesh['wide'=32,'narrow'=8] {'wide'}, dimensions={0}, use_global_device_ids=true | all-gather | bytes 540672 | tf_op jit(solution)/shard_map/all_gather | solution.py:147
  267.1 4.8 %fusion.71 = f32[256,2048]{1,0:T(8,128)} fusion(bf16[256,1024]{1,0:T(8,128)(2,1)S(1)} %all_gather.7, bf16[1024,2048]{1,0:T(8,128)(2,1)} %param.24), kind=kOutput, calls=%fused_computation.152 | convolution fusion | flops 1073741824 | bytes 6815744 | tf_op jit(solution)/shard_map/dot_general | solution.py:146
  271.9 0.0 copy-start.6
  271.9 0.0 copy-start.7
  271.9 0.0 copy-start.10
  271.9 0.0 all-reduce.2.cloned.1.call-update
  271.9 0.0 reduce-scatter.8.cloned.1.call-start
  272.0 0.6 copy-done.6
  272.6 0.0 copy-done.7
  272.6 82.2 %all-reduce.2.cloned.1.call-done = f32[256,2048]{1,0:T(8,128)} async-done(((f32[256,2048]{1,0:T(8,128)}), f32[256,2048]{1,0:T(8,128)}) %all-reduce.2.cloned.1.call-update) | async-done | bytes 2097168 | tf_op jit(solution)/shard_map/psum | solution.py:153
  354.8 0.0 copy-done.10
  354.8 0.0 copy-start.8
  354.8 6.1 %fusion.19 = f32[256,1024]{1,0:T(8,128)} fusion(bf16[2048,1024]{1,0:T(8,128)(2,1)} %param.26, f32[256,2048]{1,0:T(8,128)} %all-reduce.2.cloned.1.call-done, f32[2048]{0:T(1024)S(1)} %copy-done.10, f32[256]{0:T(256)S(1)} %bitcast.219, f32[256]{0:T(256)S(1)} %bitcast.220, f32[256]{0:T(256)S(1)} %bitcast.214, f32[256]{0:T(256)S(1)} %bitcast.215, ...), kind=kOutput, calls=%fused_computation.11 | convolution fusion | flops 1083179008 | bytes 7372800 | tf_op jit(solution)/shard_map/dot_general | solution.py:157
  360.9 0.0 reduce-scatter.8.cloned.1.call-update
  361.0 90.6 %reduce-scatter.8.cloned.1.call-done = f32[8,1024]{1,0:T(8,128)} async-done(((f32[256,1024]{1,0:T(8,128)}), f32[8,1024]{1,0:T(8,128)}) %reduce-scatter.8.cloned.1.call-update) | async-done | bytes 32784 | tf_op jit(solution)/shard_map/reduce_scatter | solution.py:156
  451.5 0.0 copy-done.8
  451.5 1.4 add_convert_fusion
  (43 shorter events, 0.2 us)
Async XLA Ops:
  6.5 114.9 %copy-start = (bf16[8,1,1024,128]{3,2,1,0:T(8,128)(2,1)S(1)}, bf16[8,1,1024,128]{3,2,1,0:T(8,128)(2,1)}, u32[]{:S(2)}) copy-start(bf16[8,1,1024,128]{3,2,1,0:T(8,128)(2,1)} %param.21) | copy-start | bytes 6291460
  6.5 25.8 %copy-start.4 = (bf16[256,128]{1,0:T(8,128)(2,1)S(1)}, bf16[256,128]{1,0:T(8,128)(2,1)}, u32[]{:S(2)}) copy-start(bf16[256,128]{1,0:T(8,128)(2,1)} %param.19) | copy-start | bytes 196612
  6.5 26.0 %copy-start.5 = (bf16[256,128]{1,0:T(8,128)(2,1)S(1)}, bf16[256,128]{1,0:T(8,128)(2,1)}, u32[]{:S(2)}) copy-start(bf16[256,128]{1,0:T(8,128)(2,1)} %param.18) | copy-start | bytes 196612
  6.5 112.8 %reduce-scatter.4.cloned.1.call-start = ((), (), s32[]{:S(2)}) async-start(), calls=%async_computation.5 | async-start | bytes 1351680 | tf_op jit(solution)/shard_map/reduce_scatter | solution.py:100
  32.6 1.5 copy-start.9
  34.0 186.1 %reduce-scatter.6.cloned.1.call-start = ((), (), s32[]{:S(2)}) async-start(), calls=%async_computation.6 | async-start | bytes 294912 | tf_op jit(solution)/shard_map/reduce_scatter | solution.py:141
  119.4 3.8 copy-start.1
  122.2 45.7 %copy-start.3 = (bf16[1024,256]{1,0:T(8,128)(2,1)S(1)}, bf16[1024,256]{1,0:T(8,128)(2,1)}, u32[]{:S(2)}) copy-start(bf16[1024,256]{1,0:T(8,128)(2,1)} %param.20) | copy-start | bytes 1572868
  123.6 62.9 %copy-start.2 = (bf16[8,8192]{1,0:T(8,128)(2,1)S(1)}, bf16[8,8192]{1,0:T(8,128)(2,1)}, u32[]{:S(2)}) copy-start(bf16[8,8192]{1,0:T(8,128)(2,1)} %param.15) | copy-start | bytes 393220
  186.4 168.4 %all-reduce.2.cloned.1.call-start = ((), (), s32[]{:S(2)}) async-start(), calls=%async_computation.7 | async-start | bytes 4194304 | tf_op jit(solution)/shard_map/psum | solution.py:153
  271.9 0.7 copy-start.6
  271.9 0.7 copy-start.7
  271.9 82.9 %copy-start.10 = (f32[2048]{0:T(1024)S(1)}, f32[2048]{0:T(1024)}, u32[]{:S(2)}) copy-start(f32[2048]{0:T(1024)} %param.25) | copy-start | bytes 24580
  271.9 179.6 %reduce-scatter.8.cloned.1.call-start = ((), (), s32[]{:S(2)}) async-start(), calls=%async_computation.8 | async-start | bytes 1081344 | tf_op jit(solution)/shard_map/reduce_scatter | solution.py:156
  354.8 96.7 %copy-start.8 = (f32[1024]{0:T(1024)S(1)}, f32[1024]{0:T(1024)}, u32[]{:S(2)}) copy-start(f32[1024]{0:T(1024)} %param.27) | copy-start | bytes 12292
Sparse Core Ops, SparseCore 0:
  34.1 85.2 reduce-scatter.3
  186.5 33.5 reduce-scatter.5
  272.0 82.7 all-reduce.1
  361.1 90.4 reduce-scatter.7
